TPU v7x, 32 devices: a whole 2x2x4 slice. The times are simulated.
32 devices in a mesh: exp: 4 (over z), row: 4 (over y, core), col: 2 (over x).
Axes of the slice: x: 2, y: 2, z: 4, core: 2. Of those that a mesh axis runs over, the one named last changes fastest.
Arguments:
- exposures: float32 [64, 128, 1024], P('exp', 'row', 'col'), may hold values from -6 to 6
- bad_pixels: int32 [64, 128, 1024], P('exp', 'row', 'col'), may hold values 0 or 1
- offsets: int32 [64, 2], P('exp'), may hold values from -8 to 8, as said below
- warp_index: int32 [64, 2], P('exp'), may hold values from 0 to 15
- blur_index: int32 [64], P('exp'), may hold values from 0 to 7
Outputs:
- residual: float32 [64, 128, 1024], P('exp', 'row', 'col')
- median_sky: float32 [128, 1024], P('row', 'col')
Inputs may be any that keep to these rules, and one draw needn't show every extreme that they name: `offsets`: in each component some exposure has the offset -8 and some has 8.
All inputs are finite; a program needn't handle non-finite values. No bound on the sum of `bad_pixels` on one device may be relied on, other than what follows from the above.
Results may differ from a plain program's by a relative error of at most 0.0003.
Values sent between devices are 32-bit elements; how exact they have to be, the bound alone decides.
No kernel may reach another device: no remote copies, remote signals or barrier semaphores. Data moves between devices by JAX's collectives and lax.ppermute only.
A program may use at most 64 MiB of HBM per device.

v0:
```python
import jax
import jax.numpy as jnp
from jax import lax
from jax.sharding import PartitionSpec as P

NFRAC = 16
NPSF = 8
PSF_RADIUS = 4
PASSES = 16
HALO = 11
sentinel = 1000000.0
half_sentinel = 500000.0
pivot_span = 16.0


def _row_halo(block, dim, width):
    count = lax.axis_size("row")
    forward = [(i, i + 1) for i in range(count - 1)]
    backward = [(target, source) for source, target in forward]
    size = block.shape[dim]
    low = lax.ppermute(lax.slice_in_dim(block, size - width, None, axis=dim), "row", forward)
    high = lax.ppermute(lax.slice_in_dim(block, 0, width, axis=dim), "row", backward)
    return jnp.concatenate([low, block, high], axis=dim)


def _col_halo(block, dim, width):
    count = lax.axis_size("col")
    size = block.shape[dim]
    right_edge = lax.slice_in_dim(block, size - width, None, axis=dim)
    left_edge = lax.slice_in_dim(block, 0, width, axis=dim)
    if count != 2:
        forward = [(i, i + 1) for i in range(count - 1)]
        backward = [(target, source) for source, target in forward]
        low = lax.ppermute(right_edge, "col", forward)
        high = lax.ppermute(left_edge, "col", backward)
        return jnp.concatenate([low, block, high], axis=dim)
    first = lax.axis_index("col") == 0
    outgoing = jnp.moveaxis(jnp.where(first, right_edge, left_edge), dim, 0)
    packed_shape = outgoing.shape
    packed = outgoing.reshape(width, -1)
    arrived = lax.ppermute(packed, "col", [(0, 1), (1, 0)])
    arrived = jnp.moveaxis(arrived.reshape(packed_shape), 0, dim)
    zeros = jnp.zeros_like(arrived)
    low = jnp.where(first, zeros, arrived)
    high = jnp.where(first, arrived, zeros)
    return jnp.concatenate([low, block, high], axis=dim)


def extended(block, row_dim, col_dim, width):
    return _col_halo(_row_halo(block, row_dim, width), col_dim, width)


def lanczos_table():
    fraction = jnp.arange(NFRAC, dtype=jnp.float32) / NFRAC
    offset_grid = jnp.arange(-2, 4, dtype=jnp.float32)
    spread = offset_grid[None, :] - fraction[:, None]
    kernel = jnp.sinc(spread) * jnp.sinc(spread / 3.0)
    return kernel / jnp.sum(kernel, axis=1, keepdims=True)


def blur_table():
    offset_grid = jnp.arange(-PSF_RADIUS, PSF_RADIUS + 1, dtype=jnp.float32)
    widths = 0.7 + 0.2 * jnp.arange(NPSF, dtype=jnp.float32)
    kernel = jnp.exp(-0.5 * (offset_grid[None, :] / widths[:, None]) ** 2)
    return kernel / jnp.sum(kernel, axis=1, keepdims=True)


def lookup(indices, entries, kernel_table):
    chooser = (indices[:, None] == lax.broadcasted_iota(jnp.int32, (1, entries), 1)).astype(
        jnp.float32
    )
    return jnp.dot(chooser, kernel_table, precision=lax.Precision.HIGHEST)


def placed_taps(weights, shifts):
    reach = 2 * HALO + 1
    positions = lax.broadcasted_iota(jnp.int32, (1, 1, reach), 2)
    tap_slot = HALO + shifts[:, None, None] + lax.broadcasted_iota(jnp.int32, (1, 6, 1), 1) - 2
    spread = (tap_slot == positions).astype(jnp.float32)
    return jnp.sum(weights[:, :, None] * spread, axis=1)


def resample_axis(stack, coefficients, out_len, which_axis):
    out_shape = list(stack.shape)
    out_shape[which_axis] = out_len
    total = jnp.zeros(tuple(out_shape), jnp.float32)
    for position in range(2 * HALO + 1):
        window = lax.slice_in_dim(stack, position, position + out_len, 1, which_axis)
        total = total + coefficients[:, position, None, None] * window
    return total


def bisect_lower(valid_count, count_below):

    def one_pass(sweep_no, bounds):
        lower_edge, upper_edge = bounds
        middle = 0.5 * (lower_edge + upper_edge)
        enough = 2.0 * count_below(middle) >= valid_count
        return (jnp.where(enough, lower_edge, middle), jnp.where(enough, middle, upper_edge))

    initial = (
        jnp.full(valid_count.shape, -pivot_span, jnp.float32),
        jnp.full(valid_count.shape, pivot_span, jnp.float32),
    )
    return lax.fori_loop(0, PASSES, one_pass, initial)[0]


def stack_median(pixel_stack):
    valid_count = jnp.sum(pixel_stack < half_sentinel, axis=0, dtype=jnp.float32)

    def count_below(middle):
        return jnp.sum(pixel_stack <= middle[None], axis=0, dtype=jnp.float32)

    lower_edge = bisect_lower(valid_count, count_below)
    return jnp.min(jnp.where(pixel_stack > lower_edge[None], pixel_stack, sentinel), axis=0)


def body(exposures, bad_pixels, offsets, warp_index, blur_index):
    group_size, row_count, col_count = exposures.shape
    kernel_table = lanczos_table()
    coef_down = placed_taps(lookup(warp_index[:, 0], NFRAC, kernel_table), offsets[:, 0])
    coef_across = placed_taps(lookup(warp_index[:, 1], NFRAC, kernel_table), offsets[:, 1])
    padded = extended(exposures, 1, 2, HALO)
    across = resample_axis(padded, coef_down, row_count, 1)
    warped = resample_axis(across, coef_across, col_count, 2)
    flagged = jnp.where(bad_pixels == 1, sentinel, warped)
    band = stack_median(lax.all_to_all(flagged, "exp", split_axis=1, concat_axis=0, tiled=True))
    groups = lax.axis_size("exp")
    median_sky = lax.all_to_all(
        jnp.tile(band, (groups, 1)), "exp", split_axis=0, concat_axis=0, tiled=True
    )
    bordered = extended(median_sky, 0, 1, PSF_RADIUS)
    blur = blur_table()
    taps = 2 * PSF_RADIUS + 1
    blurred_rows = jnp.zeros((NPSF, row_count, col_count + 2 * PSF_RADIUS), jnp.float32)
    for tap_no in range(taps):
        blurred_rows = (
            blurred_rows
            + blur[:, tap_no, None, None] * bordered[None, tap_no : tap_no + row_count, :]
        )
    smoothed = jnp.zeros((NPSF, row_count, col_count), jnp.float32)
    for tap_no in range(taps):
        smoothed = (
            smoothed + blur[:, tap_no, None, None] * blurred_rows[:, :, tap_no : tap_no + col_count]
        )
    chooser = (blur_index[:, None] == lax.broadcasted_iota(jnp.int32, (1, NPSF), 1)).astype(
        jnp.float32
    )
    sky_model = jnp.zeros((group_size, row_count, col_count), jnp.float32)
    for kernel_no in range(NPSF):
        sky_model = sky_model + chooser[:, kernel_no, None, None] * smoothed[kernel_no][None]
    residual = jnp.where(bad_pixels == 1, 0.0, warped - sky_model)
    return (residual, median_sky)


def solution(mesh):
    return jax.shard_map(
        body,
        mesh=mesh,
        in_specs=(
            P("exp", "row", "col"),
            P("exp", "row", "col"),
            P("exp", None),
            P("exp", None),
            P("exp"),
        ),
        out_specs=(P("exp", "row", "col"), P("row", "col")),
        check_vma=False,
    )
```

profile of v0, /device:TPU:0, one launch (start us, length us, event | category | flops | bytes accessed | tf_op | source)
XLA Modules:
  0.0 90.9 jit_solution(72379477720639308)
XLA Ops:
  0.6 1.3 %fusion.134 = (f32[16,11,512]{2,1,0:T(8,128)S(1)}, f32[16,11,512]{2,1,0:T(8,128)S(1)}) fusion(f32[16,32,512]{2,1,0:T(8,128)} %param.8), kind=kLoop, calls=%fused_computation.315 | loop fusion | bytes 1441792 | tf_op jit(solution)/shard_map/slice | solution.py:22
  2.0 0.2 copy.47
  2.2 3.3 %collective-permute-start = (f32[16,11,512]{2,0,1:T(8,128)S(1)}, f32[16,11,512]{2,0,1:T(8,128)}, u32[]{:S(2)}, u32[]{:S(2)}) collective-permute-start(f32[16,11,512]{2,0,1:T(8,128)S(1)} %copy.47), channel_id=1, source_target_pairs={{0,2},{2,4},{4,6},{1,3},{3,5},{5,7},{8,10},{10,12},{12,14},{9,11},... | collective-permute-start | bytes 1081352 | tf_op jit(solution)/shard_map/ppermute | solution.py:21
  5.5 0.2 copy.48
  5.7 1.3 %collective-permute-start.1 = (f32[16,11,512]{2,0,1:T(8,128)S(1)}, f32[16,11,512]{2,0,1:T(8,128)S(1)}, u32[]{:S(2)}, u32[]{:S(2)}) collective-permute-start(f32[16,11,512]{2,0,1:T(8,128)S(1)} %copy.48), channel_id=1, source_target_pairs={{2,0},{4,2},{6,4},{3,1},{5,3},{7,5},{10,8},{12,10},{14,12},{11,9},... | collective-permute-start | bytes 1081352 | tf_op jit(solution)/shard_map/ppermute | solution.py:22
  7.2 0.2 fusion.67
  7.4 0.2 fusion.66
  7.7 0.8 slice_reduce_fusion.43
  8.5 1.1 %slice_reduce_fusion.44 = (f32[16]{0:T(128)}, f32[16]{0:T(128)}, f32[16]{0:T(128)}, f32[16]{0:T(128)}, f32[16]{0:T(128)}, /*index=5*/f32[16]{0:T(128)}, f32[16]{...) fusion(f32[16,23]{1,0:T(8,128)S(1)} %select_reduce_fusion), kind=kLoop, calls=%fused_computation.204 | loop fusion | bytes 2432 | tf_op jit(solution)/shard_map/slice | solution.py:89
  9.7 1.1 %slice_reduce_fusion.45 = (f32[16]{0:T(128)S(1)}, f32[16]{0:T(128)S(1)}, f32[16]{0:T(128)}, f32[16]{0:T(128)}, f32[16]{0:T(128)}, /*index=5*/f32[16]{0:T(128)}, ...) fusion(f32[16,23]{1,0:T(8,128)S(1)} %select_reduce_fusion.1), kind=kLoop, calls=%fused_computation.205 | loop fusion | bytes 2432 | tf_op jit(solution)/shard_map/slice | solution.py:89
  10.7 1.0 %constant_dynamic-update-slice_fusion.2 = f32[16,54,512]{2,0,1:T(8,128)S(1)} fusion(f32[16,11,512]{2,0,1:T(8,128)} %collective-permute-done), kind=kLoop, calls=%fused_computation.208 | loop fusion | bytes 720896
  11.8 0.6 constant_dynamic-update-slice_fusion.1
  12.4 0.2 fusion.53
  12.6 0.3 copy.40
  13.0 2.4 %collective-permute-start.2 = (f32[11,864]{1,0:T(8,128)S(1)}, f32[11,864]{1,0:T(8,128)S(1)}, u32[]{:S(2)}, u32[]{:S(2)}) collective-permute-start(f32[11,864]{1,0:T(8,128)S(1)} %reshape.187), channel_id=1, source_target_pairs={{0,1},{1,0},{2,3},{3,2},{4,5},{5,4},{6,7},{7,6},{8,9},{9,8},{10,11... | collective-permute-start | bytes 114056 | tf_op jit(solution)/shard_map/ppermute | solution.py:41
  15.4 0.2 slice_reduce_fusion.21
  15.6 1.9 %collective-permute-done.2 = f32[11,864]{1,0:T(8,128)S(1)} collective-permute-done((f32[11,864]{1,0:T(8,128)S(1)}, f32[11,864]{1,0:T(8,128)S(1)}, u32[]{:S(2)}, u32[]{:S(2)}) %collective-permute-start.2) | collective-permute-done | bytes 38048 | tf_op jit(solution)/shard_map/ppermute | solution.py:41
  17.6 0.3 copy.42
  18.1 0.3 copy.41
  18.6 0.7 pad_maximum_fusion
  19.8 3.9 %fusion = f32[16,32,534]{2,0,1:T(8,128)S(1)} fusion(f32[16,54,534]{2,0,1:T(8,128)S(1)} %pad_maximum_fusion, f32[16]{0:T(128)S(1)} %copy-done.24, f32[16]{0:T(128)S(1)} %copy-done.25, f32[16]{0:T(128)S(1)} %copy-done.26, f32[16]{0:T(128)S(1)} %copy-done.27, f32[16]{0:T(128)S(1)} %copy-done.28, f32[16]{0:T(128)S(1)} %copy-done.29, f32[16]{0:T(128)S(1)} %copy-done.30, ...), kind=kLoop, calls=%fused_computation.8 | loop fusion | flops 12303360 | bytes 26248640 | tf_op jit(solution)/shard_map/add | solution.py:89
  23.8 7.0 %broadcast_select_fusion = (f32[16,32,512]{2,0,1:T(8,128)}, f32[16,32,512]{2,0,1:T(8,128)S(1)}, pred[16,32,512]{2,0,1:T(8,128)(4,1)S(1)}) fusion(f32[16,32,534]{2,0,1:T(8,128)S(1)} %fusion, f32[16]{0:T(128)S(1)} %get-tuple-element.56, f32[16]{0:T(128)S(1)} %copy-done.2, f32[16]{0:T(128)S(1)} %copy-done.3, f32[16]{0:T(128)S(1)} %copy-done.4, ...), kind=kLoop, calls=%fused_computation.119 | loop fusion | flops 12320768 | bytes 27526592 | tf_op jit(solution)/shard_map/jit(_where)/select_n | solution.py:126
  30.8 5.4 %all-to-all-start = ((f32[16,32,512]{2,0,1:T(8,128)}), f32[16,32,512]{2,0,1:T(8,128)S(1)}, u32[]{:S(2)}, u32[]{:S(2)}) async-start(f32[16,32,512]{2,0,1:T(8,128)} %get-tuple-element.113), calls=%async_computation | async-start | bytes 2097152 | tf_op jit(solution)/shard_map/all_to_all | solution.py:127
  36.4 26.2 %all-to-all-done = f32[16,32,512]{2,0,1:T(8,128)S(1)} async-done(((f32[16,32,512]{2,0,1:T(8,128)}), f32[16,32,512]{2,0,1:T(8,128)S(1)}, u32[]{:S(2)}, u32[]{:S(2)}) %all-to-all-start) | async-done | bytes 1048608 | tf_op jit(solution)/shard_map/all_to_all | solution.py:127
  62.6 0.6 copy.43
  63.2 0.1 convert_reduce_fusion.1
  63.4 3.6 %while.13 = (s32[]{:T(128)}, f32[8,512]{1,0:T(8,128)S(1)}, f32[8,512]{1,0:T(8,128)S(1)}, f32[64,8,512]{2,1,0:T(8,128)S(1)}, f32[8,512]{1,0:T(8,128)S(1)}, /*index=5*/s32[]{:T(128)}, s32[]{:T(128)}) while((s32[]{:T(128)}, f32[8,512]{1,0:T(8,128)S(1)}, f32[8,512]{1,0:T(8,128)S(1)}, f32[64,8,512]{2,1,0:T(8,128)S(1)}, ...), condition=%wide.region_7.9_spmd.clone, body=%wide.region_5.8_spmd.clone.sunk | while | flops 1110019 | bytes 1302625 | solution.py:105
  63.4 0.1 convert_reduce_fusion.3
  63.6 0.1 convert_reduce_fusion.3
  63.9 0.1 convert_reduce_fusion.3
  64.1 0.1 convert_reduce_fusion.3
  64.3 0.1 convert_reduce_fusion.3
  64.5 0.1 convert_reduce_fusion.3
  64.8 0.1 convert_reduce_fusion.3
  67.0 0.2 fusion.22
  67.2 0.6 tile.2
  67.8 3.3 %all-to-all-start.1 = ((f32[4,8,512]{2,1,0:T(8,128)}), f32[4,8,512]{2,1,0:T(8,128)S(1)}, u32[]{:S(2)}, u32[]{:S(2)}) async-start(f32[4,8,512]{2,1,0:T(8,128)} %tile.2), calls=%async_computation.1 | async-start | bytes 131072 | tf_op jit(solution)/shard_map/all_to_all | solution.py:129
  71.1 5.8 %all-to-all-done.1 = f32[4,8,512]{2,1,0:T(8,128)S(1)} async-done(((f32[4,8,512]{2,1,0:T(8,128)}), f32[4,8,512]{2,1,0:T(8,128)S(1)}, u32[]{:S(2)}, u32[]{:S(2)}) %all-to-all-start.1) | async-done | bytes 65568 | tf_op jit(solution)/shard_map/all_to_all | solution.py:129
  76.9 1.3 %collective-permute-start.4 = (f32[4,512]{1,0:T(4,128)S(1)}, f32[4,512]{1,0:T(4,128)S(1)}, u32[]{:S(2)}, u32[]{:S(2)}) collective-permute-start(f32[4,512]{1,0:T(4,128)S(1)} %get-tuple-element.136), channel_id=1, source_target_pairs={{2,0},{4,2},{6,4},{3,1},{5,3},{7,5},{10,8},{12,10},{14,12},{11,9},... | collective-permute-start | bytes 24584 | tf_op jit(solution)/shard_map/ppermute | solution.py:22
  78.2 3.2 %collective-permute-start.3 = (f32[4,512]{1,0:T(4,128)S(1)}, f32[4,512]{1,0:T(4,128)S(1)}, u32[]{:S(2)}, u32[]{:S(2)}) collective-permute-start(f32[4,512]{1,0:T(4,128)S(1)} %get-tuple-element.135), channel_id=1, source_target_pairs={{0,2},{2,4},{4,6},{1,3},{3,5},{5,7},{8,10},{10,12},{12,14},{9,11},... | collective-permute-start | bytes 24584 | tf_op jit(solution)/shard_map/ppermute | solution.py:21
  81.5 0.6 collective-permute-done.3
  82.1 1.5 %collective-permute-start.5 = (f32[4,40]{0,1:T(8,128)S(1)}, f32[4,40]{0,1:T(8,128)S(1)}, u32[]{:S(2)}, u32[]{:S(2)}) collective-permute-start(f32[4,40]{0,1:T(8,128)S(1)} %fusion.55), channel_id=1, source_target_pairs={{0,1},{1,0},{2,3},{3,2},{4,5},{5,4},{6,7},{7,6},{8,9},{9,8},{10,11... | collective-permute-start | bytes 1928 | tf_op jit(solution)/shard_map/ppermute | solution.py:41
  83.7 2.3 %collective-permute-done.5 = f32[4,40]{0,1:T(8,128)S(1)} collective-permute-done((f32[4,40]{0,1:T(8,128)S(1)}, f32[4,40]{0,1:T(8,128)S(1)}, u32[]{:S(2)}, u32[]{:S(2)}) %collective-permute-start.5) | collective-permute-done | bytes 672 | tf_op jit(solution)/shard_map/ppermute | solution.py:41
  86.1 0.6 multiply_add_fusion
  86.7 1.3 %fusion.45 = f32[8,32,512]{2,1,0:T(8,128)S(1)} fusion(f32[8,32,520]{2,1,0:T(8,128)S(1)} %multiply_add_fusion, f32[8]{0:T(128)S(1)} %get-tuple-element.142, f32[8]{0:T(128)S(1)} %get-tuple-element.143, f32[8]{0:T(128)S(1)} %get-tuple-element.144, f32[8]{0:T(128)S(1)} %get-tuple-element.145, f32[8]{0:T(128)S(1)} %get-tuple-element.146, ...), kind=kLoop, calls=%fused_computation.103 | loop fusion | flops 2228224 | bytes 5243168 | tf_op jit(solution)/shard_map/add | solution.py:144
  88.0 0.7 subtract_select_fusion
  88.7 1.6 %copy.44 = f32[16,32,512]{2,1,0:T(8,128)} copy(f32[16,32,512]{2,0,1:T(8,128)S(1)} %subtract_select_fusion) | data formatting | bytes 2097152
  90.3 0.6 copy.62
  (192 shorter events, 3.3 us)
Async XLA Ops:
  2.0 5.1 %copy-start.41 = (s32[16,2]{0,1:T(2,128)S(1)}, s32[16,2]{0,1:T(2,128)}, u32[]{:S(2)}) copy-start(s32[16,2]{0,1:T(2,128)} %param.11) | copy-start | bytes 388
  2.0 5.1 %copy-start.42 = (s32[16,2]{0,1:T(2,128)S(1)}, s32[16,2]{0,1:T(2,128)}, u32[]{:S(2)}) copy-start(s32[16,2]{0,1:T(2,128)} %param.10) | copy-start | bytes 388
  2.2 9.6 %copy-start = (f32[16,32,512]{2,1,0:T(8,128)S(1)}, f32[16,32,512]{2,1,0:T(8,128)}, u32[]{:S(2)}) copy-start(f32[16,32,512]{2,1,0:T(8,128)} %param.8) | copy-start | bytes 3145732
  2.2 8.5 %collective-permute-start = (f32[16,11,512]{2,0,1:T(8,128)S(1)}, f32[16,11,512]{2,0,1:T(8,128)}, u32[]{:S(2)}, u32[]{:S(2)}) collective-permute-start(f32[16,11,512]{2,0,1:T(8,128)S(1)} %copy.47), channel_id=1, source_target_pairs={{0,2},{2,4},{4,6},{1,3},{3,5},{5,7},{8,10},{10,12},{12,14},{9,11},... | collective-permute-start | bytes 1081352 | tf_op jit(solution)/shard_map/ppermute | solution.py:21
  5.7 6.7 %collective-permute-start.1 = (f32[16,11,512]{2,0,1:T(8,128)S(1)}, f32[16,11,512]{2,0,1:T(8,128)S(1)}, u32[]{:S(2)}, u32[]{:S(2)}) collective-permute-start(f32[16,11,512]{2,0,1:T(8,128)S(1)} %copy.48), channel_id=1, source_target_pairs={{2,0},{4,2},{6,4},{3,1},{5,3},{7,5},{10,8},{12,10},{14,12},{11,9},... | collective-permute-start | bytes 1081352 | tf_op jit(solution)/shard_map/ppermute | solution.py:22
  13.0 4.5 %collective-permute-start.2 = (f32[11,864]{1,0:T(8,128)S(1)}, f32[11,864]{1,0:T(8,128)S(1)}, u32[]{:S(2)}, u32[]{:S(2)}) collective-permute-start(f32[11,864]{1,0:T(8,128)S(1)} %reshape.187), channel_id=1, source_target_pairs={{0,1},{1,0},{2,3},{3,2},{4,5},{5,4},{6,7},{7,6},{8,9},{9,8},{10,11... | collective-permute-start | bytes 114056 | tf_op jit(solution)/shard_map/ppermute | solution.py:41
  18.4 1.0 %copy-start.19 = (f32[16]{0:T(128)S(1)}, f32[16]{0:T(128)}, u32[]{:S(2)}) copy-start(f32[16]{0:T(128)} %get-tuple-element.97) | copy-start | bytes 196
  18.4 1.0 %copy-start.20 = (f32[16]{0:T(128)S(1)}, f32[16]{0:T(128)}, u32[]{:S(2)}) copy-start(f32[16]{0:T(128)} %get-tuple-element.98) | copy-start | bytes 196
  18.4 1.0 %copy-start.21 = (f32[16]{0:T(128)S(1)}, f32[16]{0:T(128)}, u32[]{:S(2)}) copy-start(f32[16]{0:T(128)} %get-tuple-element.99) | copy-start | bytes 196
  18.4 1.0 %copy-start.22 = (f32[16]{0:T(128)S(1)}, f32[16]{0:T(128)}, u32[]{:S(2)}) copy-start(f32[16]{0:T(128)} %get-tuple-element.100) | copy-start | bytes 196
  18.4 1.0 %copy-start.23 = (f32[16]{0:T(128)S(1)}, f32[16]{0:T(128)}, u32[]{:S(2)}) copy-start(f32[16]{0:T(128)} %get-tuple-element.78) | copy-start | bytes 196
  18.4 1.0 %copy-start.24 = (f32[16]{0:T(128)S(1)}, f32[16]{0:T(128)}, u32[]{:S(2)}) copy-start(f32[16]{0:T(128)} %get-tuple-element.79) | copy-start | bytes 196
  18.5 1.0 %copy-start.25 = (f32[16]{0:T(128)S(1)}, f32[16]{0:T(128)}, u32[]{:S(2)}) copy-start(f32[16]{0:T(128)} %get-tuple-element.80) | copy-start | bytes 196
  18.5 1.0 %copy-start.26 = (f32[16]{0:T(128)S(1)}, f32[16]{0:T(128)}, u32[]{:S(2)}) copy-start(f32[16]{0:T(128)} %get-tuple-element.81) | copy-start | bytes 196
  18.5 1.0 %copy-start.27 = (f32[16]{0:T(128)S(1)}, f32[16]{0:T(128)}, u32[]{:S(2)}) copy-start(f32[16]{0:T(128)} %get-tuple-element.82) | copy-start | bytes 196
  18.5 1.0 %copy-start.28 = (f32[16]{0:T(128)S(1)}, f32[16]{0:T(128)}, u32[]{:S(2)}) copy-start(f32[16]{0:T(128)} %get-tuple-element.83) | copy-start | bytes 196
  18.5 1.0 %copy-start.29 = (f32[16]{0:T(128)S(1)}, f32[16]{0:T(128)}, u32[]{:S(2)}) copy-start(f32[16]{0:T(128)} %get-tuple-element.84) | copy-start | bytes 196
  18.5 1.0 %copy-start.30 = (f32[16]{0:T(128)S(1)}, f32[16]{0:T(128)}, u32[]{:S(2)}) copy-start(f32[16]{0:T(128)} %get-tuple-element.85) | copy-start | bytes 196
  18.5 1.0 %copy-start.31 = (f32[16]{0:T(128)S(1)}, f32[16]{0:T(128)}, u32[]{:S(2)}) copy-start(f32[16]{0:T(128)} %get-tuple-element.86) | copy-start | bytes 196
  18.5 1.0 %copy-start.32 = (f32[16]{0:T(128)S(1)}, f32[16]{0:T(128)}, u32[]{:S(2)}) copy-start(f32[16]{0:T(128)} %get-tuple-element.87) | copy-start | bytes 196
  18.5 1.0 %copy-start.33 = (f32[16]{0:T(128)S(1)}, f32[16]{0:T(128)}, u32[]{:S(2)}) copy-start(f32[16]{0:T(128)} %get-tuple-element.88) | copy-start | bytes 196
  18.5 1.0 %copy-start.34 = (f32[16]{0:T(128)S(1)}, f32[16]{0:T(128)}, u32[]{:S(2)}) copy-start(f32[16]{0:T(128)} %get-tuple-element.89) | copy-start | bytes 196
  18.6 1.0 %copy-start.35 = (f32[16]{0:T(128)S(1)}, f32[16]{0:T(128)}, u32[]{:S(2)}) copy-start(f32[16]{0:T(128)} %get-tuple-element.90) | copy-start | bytes 196
  18.6 1.0 %copy-start.36 = (f32[16]{0:T(128)S(1)}, f32[16]{0:T(128)}, u32[]{:S(2)}) copy-start(f32[16]{0:T(128)} %get-tuple-element.91) | copy-start | bytes 196
  19.6 4.0 %copy-start.1 = (s32[16,32,512]{2,1,0:T(8,128)S(1)}, s32[16,32,512]{2,1,0:T(8,128)}, u32[]{:S(2)}) copy-start(s32[16,32,512]{2,1,0:T(8,128)} %param.9) | copy-start | bytes 3145732
  19.6 4.0 %copy-start.2 = (f32[16]{0:T(128)S(1)}, f32[16]{0:T(128)}, u32[]{:S(2)}) copy-start(f32[16]{0:T(128)} %get-tuple-element.57) | copy-start | bytes 196
  19.6 4.0 %copy-start.3 = (f32[16]{0:T(128)S(1)}, f32[16]{0:T(128)}, u32[]{:S(2)}) copy-start(f32[16]{0:T(128)} %get-tuple-element.58) | copy-start | bytes 196
  19.6 4.0 %copy-start.4 = (f32[16]{0:T(128)S(1)}, f32[16]{0:T(128)}, u32[]{:S(2)}) copy-start(f32[16]{0:T(128)} %get-tuple-element.59) | copy-start | bytes 196
  19.6 4.0 %copy-start.5 = (f32[16]{0:T(128)S(1)}, f32[16]{0:T(128)}, u32[]{:S(2)}) copy-start(f32[16]{0:T(128)} %get-tuple-element.60) | copy-start | bytes 196
  19.6 4.0 %copy-start.6 = (f32[16]{0:T(128)S(1)}, f32[16]{0:T(128)}, u32[]{:S(2)}) copy-start(f32[16]{0:T(128)} %get-tuple-element.61) | copy-start | bytes 196
  19.6 4.0 %copy-start.7 = (f32[16]{0:T(128)S(1)}, f32[16]{0:T(128)}, u32[]{:S(2)}) copy-start(f32[16]{0:T(128)} %get-tuple-element.62) | copy-start | bytes 196
  19.7 4.0 %copy-start.8 = (f32[16]{0:T(128)S(1)}, f32[16]{0:T(128)}, u32[]{:S(2)}) copy-start(f32[16]{0:T(128)} %get-tuple-element.63) | copy-start | bytes 196
  19.7 4.0 %copy-start.9 = (f32[16]{0:T(128)S(1)}, f32[16]{0:T(128)}, u32[]{:S(2)}) copy-start(f32[16]{0:T(128)} %get-tuple-element.64) | copy-start | bytes 196
  19.7 4.0 %copy-start.10 = (f32[16]{0:T(128)S(1)}, f32[16]{0:T(128)}, u32[]{:S(2)}) copy-start(f32[16]{0:T(128)} %get-tuple-element.65) | copy-start | bytes 196
  19.7 4.0 %copy-start.11 = (f32[16]{0:T(128)S(1)}, f32[16]{0:T(128)}, u32[]{:S(2)}) copy-start(f32[16]{0:T(128)} %get-tuple-element.66) | copy-start | bytes 196
  19.7 4.0 %copy-start.12 = (f32[16]{0:T(128)S(1)}, f32[16]{0:T(128)}, u32[]{:S(2)}) copy-start(f32[16]{0:T(128)} %get-tuple-element.67) | copy-start | bytes 196
  19.7 4.0 %copy-start.13 = (f32[16]{0:T(128)S(1)}, f32[16]{0:T(128)}, u32[]{:S(2)}) copy-start(f32[16]{0:T(128)} %get-tuple-element.68) | copy-start | bytes 196
  19.7 4.0 %copy-start.14 = (f32[16]{0:T(128)S(1)}, f32[16]{0:T(128)}, u32[]{:S(2)}) copy-start(f32[16]{0:T(128)} %get-tuple-element.69) | copy-start | bytes 196
  19.7 4.0 %copy-start.15 = (f32[16]{0:T(128)S(1)}, f32[16]{0:T(128)}, u32[]{:S(2)}) copy-start(f32[16]{0:T(128)} %get-tuple-element.70) | copy-start | bytes 196
  19.7 4.0 %copy-start.16 = (f32[16]{0:T(128)S(1)}, f32[16]{0:T(128)}, u32[]{:S(2)}) copy-start(f32[16]{0:T(128)} %get-tuple-element.71) | copy-start | bytes 196
  19.7 4.0 %copy-start.17 = (f32[16]{0:T(128)S(1)}, f32[16]{0:T(128)}, u32[]{:S(2)}) copy-start(f32[16]{0:T(128)} %get-tuple-element.72) | copy-start | bytes 196
  19.8 4.0 %copy-start.18 = (f32[16]{0:T(128)S(1)}, f32[16]{0:T(128)}, u32[]{:S(2)}) copy-start(f32[16]{0:T(128)} %get-tuple-element.73) | copy-start | bytes 196
  30.8 31.8 %all-to-all-start = ((f32[16,32,512]{2,0,1:T(8,128)}), f32[16,32,512]{2,0,1:T(8,128)S(1)}, u32[]{:S(2)}, u32[]{:S(2)}) async-start(f32[16,32,512]{2,0,1:T(8,128)} %get-tuple-element.113), calls=%async_computation | async-start | bytes 2097152 | tf_op jit(solution)/shard_map/all_to_all | solution.py:127
  67.0 14.4 %copy-start.43 = (s32[16]{0:T(128)S(1)}, s32[16]{0:T(128)}, u32[]{:S(2)}) copy-start(s32[16]{0:T(128)} %param.12) | copy-start | bytes 196
  67.8 9.1 %all-to-all-start.1 = ((f32[4,8,512]{2,1,0:T(8,128)}), f32[4,8,512]{2,1,0:T(8,128)S(1)}, u32[]{:S(2)}, u32[]{:S(2)}) async-start(f32[4,8,512]{2,1,0:T(8,128)} %tile.2), calls=%async_computation.1 | async-start | bytes 131072 | tf_op jit(solution)/shard_map/all_to_all | solution.py:129
  76.9 4.5 %collective-permute-start.4 = (f32[4,512]{1,0:T(4,128)S(1)}, f32[4,512]{1,0:T(4,128)S(1)}, u32[]{:S(2)}, u32[]{:S(2)}) collective-permute-start(f32[4,512]{1,0:T(4,128)S(1)} %get-tuple-element.136), channel_id=1, source_target_pairs={{2,0},{4,2},{6,4},{3,1},{5,3},{7,5},{10,8},{12,10},{14,12},{11,9},... | collective-permute-start | bytes 24584 | tf_op jit(solution)/shard_map/ppermute | solution.py:22
  78.2 3.8 %collective-permute-start.3 = (f32[4,512]{1,0:T(4,128)S(1)}, f32[4,512]{1,0:T(4,128)S(1)}, u32[]{:S(2)}, u32[]{:S(2)}) collective-permute-start(f32[4,512]{1,0:T(4,128)S(1)} %get-tuple-element.135), channel_id=1, source_target_pairs={{0,2},{2,4},{4,6},{1,3},{3,5},{5,7},{8,10},{10,12},{12,14},{9,11},... | collective-permute-start | bytes 24584 | tf_op jit(solution)/shard_map/ppermute | solution.py:21
  82.1 3.8 %collective-permute-start.5 = (f32[4,40]{0,1:T(8,128)S(1)}, f32[4,40]{0,1:T(8,128)S(1)}, u32[]{:S(2)}, u32[]{:S(2)}) collective-permute-start(f32[4,40]{0,1:T(8,128)S(1)} %fusion.55), channel_id=1, source_target_pairs={{0,1},{1,0},{2,3},{3,2},{4,5},{5,4},{6,7},{7,6},{8,9},{9,8},{10,11... | collective-permute-start | bytes 1928 | tf_op jit(solution)/shard_map/ppermute | solution.py:41
  (4 other events, 3.9 us)
where the time goes:
time: 91.4 us; the launch traced here: 90.9 us
  waiting for transfers between devices  36.9 us (40%)
  starting transfers between devices  21.6 us (24%)
  other arithmetic  18.2 us (20%)
  local copies, waits for them, and re-layouts  11.5 us (13%)
  between operations  1.6 us (2%)
    all_to_all x1, waiting for transfers between devices, body(): lax.all_to_all(flagged, 'exp', split_axis=1, concat_axis=0, tiled=True)  26.2 us
    select_n x1, other arithmetic, body(): flagged = jnp.where(bad_pixels == 1, sentinel, warped)  6.99 us
    ppermute x2, starting transfers between devices, _row_halo(): lax.ppermute(lax.slice_in_dim(block, size - width, None, axis=dim), 'row'...  6.48 us
    all_to_all x1, waiting for transfers between devices, body(): lax.all_to_all(jnp.tile(band, (groups, 1)), 'exp', split_axis=0, concat_a...  5.8 us
    all_to_all x1, starting transfers between devices, body(): lax.all_to_all(flagged, 'exp', split_axis=1, concat_axis=0, tiled=True)  5.4 us
    unnamed x94, local copies, waits for them, and re-layouts  4.46 us
    ppermute x2, waiting for transfers between devices, _col_halo(): arrived = lax.ppermute(packed, 'col', [(0, 1), (1, 0)])  4.23 us
    ppermute x2, starting transfers between devices, _col_halo(): arrived = lax.ppermute(packed, 'col', [(0, 1), (1, 0)])  3.87 us
  transfers between devices with their start and end apart: 8, of which 5 were waited for; matrix products, arithmetic and copies ran while one was open for 7% of the time, Pallas kernels for 0%

commit v1 on v0

--- a/solution.py
+++ b/solution.py
@@ -11,6 +11,29 @@
 sentinel = 1000000.0
 half_sentinel = 500000.0
 pivot_span = 16.0
+
+
+def split_up(x, dim, devices):
+    shape = x.shape
+    tiles = x.reshape(*shape[:dim], devices, shape[dim] // devices, *shape[dim + 1 :])
+    return jnp.moveaxis(tiles, dim, 0)
+
+
+def joined_along(tiles, dim):
+    tiles = jnp.moveaxis(tiles, 0, dim)
+    shape = tiles.shape
+    return tiles.reshape(*shape[:dim], shape[dim] * shape[dim + 1], *shape[dim + 2 :])
+
+
+def pairwise_exchange(x, axis, split_dim, concat_dim):
+    peers, position = (lax.axis_size(axis), lax.axis_index(axis))
+    blocks = split_up(x, split_dim, peers)
+    outs = [blocks[position]]
+    for step in range(1, peers):
+        sent = blocks[position ^ step]
+        outs.append(lax.ppermute(sent, axis, [(i, i ^ step) for i in range(peers)]))
+    blocks = jnp.stack(outs)[position ^ jnp.arange(peers)]
+    return joined_along(blocks, concat_dim)
 
 
 def _row_halo(block, dim, width):
@@ -124,7 +147,7 @@
     across = resample_axis(padded, coef_down, row_count, 1)
     warped = resample_axis(across, coef_across, col_count, 2)
     flagged = jnp.where(bad_pixels == 1, sentinel, warped)
-    band = stack_median(lax.all_to_all(flagged, "exp", split_axis=1, concat_axis=0, tiled=True))
+    band = stack_median(pairwise_exchange(flagged, "exp", 1, 0))
     groups = lax.axis_size("exp")
     median_sky = lax.all_to_all(
         jnp.tile(band, (groups, 1)), "exp", split_axis=0, concat_axis=0, tiled=True

time: 91.4 us -> 85.6 us (0.937)
  local copies, waits for them, and re-layouts: 11.5 us -> 6.85 us
  waiting for transfers between devices: 36.9 us -> 33.2 us
  other arithmetic: 18.2 us -> 21.7 us
    all_to_all x1 -> x0, waiting for transfers between devices: 26.2 us -> none  [body(): lax.all_to_all(flagged, 'exp', split_axis=1, concat_axis=0, tiled=True)]
    ppermute x0 -> x3, waiting for transfers between devices: none -> 22 us  [pairwise_exchange(): outs.append(lax.ppermute(sent, axis, [(i, i ^ step) for i in range(peers)]))]
    reshape x0 -> x1, other arithmetic: none -> 7.57 us  [split_up(): x.reshape(*shape[:dim], devices, shape[dim] // devices, *shape[dim + 1:])]
    select_n x1, other arithmetic: 6.99 us -> 0.01 us  [pairwise_exchange(): blocks = jnp.stack(outs)[position ^ jnp.arange(peers)]]
    all_to_all x1 -> x0, starting transfers between devices: 5.4 us -> none  [body(): lax.all_to_all(flagged, 'exp', split_axis=1, concat_axis=0, tiled=True)]
    ppermute x0 -> x3, starting transfers between devices: none -> 4.84 us  [pairwise_exchange(): outs.append(lax.ppermute(sent, axis, [(i, i ^ step) for i in range(peers)]))]
    unnamed x94 -> x17, local copies, waits for them, and re-layouts: 4.46 us -> 1.44 us
    slice x4, local copies, waits for them, and re-layouts: 3.13 us -> 1.41 us  [resample_axis(): total = total + coefficients[:, position, None, None] * window]
  transfers between devices with their start and end apart: 8 -> 10, of which waited for: 5 -> 6; matrix products, arithmetic and copies ran while one was open for 7% -> 3% of each run, Pallas kernels for 0% -> 0%
where the time goes in v1:
time: 85.6 us; the launch traced here: 85.1 us
  waiting for transfers between devices  33.2 us (39%)
  other arithmetic  21.7 us (25%)
  starting transfers between devices  21.3 us (25%)
  local copies, waits for them, and re-layouts  6.85 us (8%)
  between operations  1 us (1%)
    ppermute x3, waiting for transfers between devices, pairwise_exchange(): outs.append(lax.ppermute(sent, axis, [(i, i ^ step) for i in range(peers)]))  22 us
    reshape x1, other arithmetic, split_up(): x.reshape(*shape[:dim], devices, shape[dim] // devices, *shape[dim + 1:])  7.57 us
    ppermute x2, starting transfers between devices, _row_halo(): lax.ppermute(lax.slice_in_dim(block, size - width, None, axis=dim), 'row'...  6.27 us
    all_to_all x1, waiting for transfers between devices, body(): lax.all_to_all(jnp.tile(band, (groups, 1)), 'exp', split_axis=0, concat_a...  5.86 us
    ppermute x3, starting transfers between devices, pairwise_exchange(): outs.append(lax.ppermute(sent, axis, [(i, i ^ step) for i in range(peers)]))  4.84 us
    ppermute x2, waiting for transfers between devices, _col_halo(): arrived = lax.ppermute(packed, 'col', [(0, 1), (1, 0)])  4.66 us
    ppermute x2, starting transfers between devices, _col_halo(): arrived = lax.ppermute(packed, 'col', [(0, 1), (1, 0)])  4.31 us
    add x1, other arithmetic, resample_axis(): total = total + coefficients[:, position, None, None] * window  4.15 us
  transfers between devices with their start and end apart: 10, of which 6 were waited for; matrix products, arithmetic and copies ran while one was open for 3% of the time, Pallas kernels for 0%

profile of v1, /device:TPU:0, one launch (start us, length us, event | category | flops | bytes accessed | tf_op | source)
XLA Modules:
  0.0 85.1 jit_solution(17753371791605788489)
XLA Ops:
  0.7 1.4 %fusion.136 = (f32[16,11,512]{2,1,0:T(8,128)S(1)}, f32[16,11,512]{2,1,0:T(8,128)S(1)}) fusion(f32[16,32,512]{2,1,0:T(8,128)} %param.8), kind=kLoop, calls=%fused_computation.323 | loop fusion | bytes 1441792 | tf_op jit(solution)/shard_map/slice | solution.py:44
  2.1 1.3 %collective-permute-start.1 = (f32[16,11,512]{2,1,0:T(8,128)S(1)}, f32[16,11,512]{2,1,0:T(8,128)S(1)}, u32[]{:S(2)}, u32[]{:S(2)}) collective-permute-start(f32[16,11,512]{2,1,0:T(8,128)S(1)} %get-tuple-element.115), channel_id=1, source_target_pairs={{2,0},{4,2},{6,4},{3,1},{5,3},{7,5},{10,8},{12,10},{14,12},{11,9},... | collective-permute-start | bytes 1081352 | tf_op jit(solution)/shard_map/ppermute | solution.py:45
  3.4 3.1 %collective-permute-start = (f32[16,11,512]{2,1,0:T(8,128)S(1)}, f32[16,11,512]{2,1,0:T(8,128)S(1)}, u32[]{:S(2)}, u32[]{:S(2)}) collective-permute-start(f32[16,11,512]{2,1,0:T(8,128)S(1)} %get-tuple-element.114), channel_id=1, source_target_pairs={{0,2},{2,4},{4,6},{1,3},{3,5},{5,7},{8,10},{10,12},{12,14},{9,11},... | collective-permute-start | bytes 1081352 | tf_op jit(solution)/shard_map/ppermute | solution.py:44
  6.6 0.2 fusion.68
  7.0 0.2 slice_reduce_fusion.43
  7.2 0.2 fusion.67
  7.5 0.2 slice_reduce_fusion.21
  7.8 0.5 slice_reduce_fusion.44
  8.3 0.5 slice_reduce_fusion.45
  8.9 0.2 fusion.54
  9.1 0.2 copy.17
  9.4 3.0 %collective-permute-start.2 = (f32[11,864]{1,0:T(8,128)S(1)}, f32[11,864]{1,0:T(8,128)S(1)}, u32[]{:S(2)}, u32[]{:S(2)}) collective-permute-start(f32[11,864]{1,0:T(8,128)S(1)} %reshape.216), channel_id=1, source_target_pairs={{0,1},{1,0},{2,3},{3,2},{4,5},{5,4},{6,7},{7,6},{8,9},{9,8},{10,11... | collective-permute-start | bytes 114056 | tf_op jit(solution)/shard_map/ppermute | solution.py:64
  12.5 2.2 %collective-permute-done.2 = f32[11,864]{1,0:T(8,128)S(1)} collective-permute-done((f32[11,864]{1,0:T(8,128)S(1)}, f32[11,864]{1,0:T(8,128)S(1)}, u32[]{:S(2)}, u32[]{:S(2)}) %collective-permute-start.2) | collective-permute-done | bytes 38048 | tf_op jit(solution)/shard_map/ppermute | solution.py:64
  14.7 0.3 copy.19
  15.1 0.3 copy.18
  15.4 1.0 %pad_maximum_fusion = f32[16,54,534]{2,1,0:T(8,128)S(1)} fusion(f32[16,54,11]{2,1,0:T(8,128)S(1)} %copy.19, f32[16,11,512]{2,1,0:T(8,128)S(1)} %collective-permute-done.1, f32[16,32,512]{2,1,0:T(8,128)S(1)} %copy-done, f32[16,11,512]{2,1,0:T(8,128)S(1)} %collective-permute-done, f32[16,54,11]{2,1,0:T(8,128)S(1)} %copy.18), kind=kLoop, calls=%fused_computation.7 | loop fusion | flops 1845504 | bytes 3691008 | tf_op jit(solution)/shard_map/concatenate | solution.py:69
  16.5 4.1 %fusion = f32[16,32,534]{2,1,0:T(8,128)S(1)} fusion(f32[16,54,534]{2,1,0:T(8,128)S(1)} %pad_maximum_fusion, f32[16]{0:T(128)S(1)} %get-tuple-element.73, f32[16]{0:T(128)S(1)} %get-tuple-element.74, f32[16]{0:T(128)S(1)} %get-tuple-element.75, f32[16]{0:T(128)S(1)} %get-tuple-element.76, f32[16]{0:T(128)S(1)} %get-tuple-element.77, ...), kind=kLoop, calls=%fused_computation.9 | loop fusion | flops 12303360 | bytes 26248640 | tf_op jit(solution)/shard_map/add | solution.py:112
  20.6 7.6 %select_bitcast_fusion = (f32[16,4,8,512]{3,2,1,0:T(8,128)S(1)}, f32[16,32,512]{2,1,0:T(8,128)S(1)}, pred[16,32,512]{2,1,0:T(8,128)(4,1)S(1)}) fusion(f32[16,32,534]{2,1,0:T(8,128)S(1)} %fusion, f32[16]{0:T(128)S(1)} %get-tuple-element.50, f32[16]{0:T(128)S(1)} %get-tuple-element.51, f32[16]{0:T(128)S(1)} %get-tuple-element.52, ...), kind=kLoop, calls=%fused_computation.102 | loop fusion | flops 12320768 | bytes 27526592 | tf_op jit(solution)/shard_map/reshape | solution.py:18
  28.3 4.2 %collective-permute-start.5 = (f32[16,8,512]{2,1,0:T(8,128)S(1)}, f32[16,8,512]{2,1,0:T(8,128)S(1)}, u32[]{:S(2)}, u32[]{:S(2)}) collective-permute-start(f32[16,8,512]{2,1,0:T(8,128)S(1)} %get-tuple-element.111), channel_id=1, source_target_pairs={{0,24},{8,16},{16,8},{24,0},{1,25},{9,17},{17,9},{25,1},{2,26},{10... | collective-permute-start | bytes 786440 | tf_op jit(solution)/shard_map/ppermute | solution.py:34
  32.5 0.6 collective-permute-start.3
  33.2 3.8 %collective-permute-done.5 = f32[16,8,512]{2,1,0:T(8,128)S(1)} collective-permute-done((f32[16,8,512]{2,1,0:T(8,128)S(1)}, f32[16,8,512]{2,1,0:T(8,128)S(1)}, u32[]{:S(2)}, u32[]{:S(2)}) %collective-permute-start.5) | collective-permute-done | bytes 262176 | tf_op jit(solution)/shard_map/ppermute | solution.py:34
  37.0 18.2 %collective-permute-done.4 = f32[16,8,512]{2,1,0:T(8,128)S(1)} collective-permute-done((f32[16,8,512]{2,1,0:T(8,128)S(1)}, f32[16,8,512]{2,1,0:T(8,128)S(1)}, u32[]{:S(2)}, u32[]{:S(2)}) %collective-permute-start.4) | collective-permute-done | bytes 262176 | tf_op jit(solution)/shard_map/ppermute | solution.py:34
  55.3 0.7 copy-done.3
  56.1 1.2 %pad_maximum_fusion.1 = f32[4,16,8,512]{3,2,1,0:T(8,128)S(1)} fusion(f32[1,16,8,512]{3,2,1,0:T(8,128)} %bitcast.93, f32[1,16,8,512]{3,2,1,0:T(8,128)} %bitcast.94, f32[1,16,8,512]{3,2,1,0:T(8,128)} %bitcast.95, f32[1,16,8,512]{3,2,1,0:T(8,128)S(1)} %get-tuple-element.110), kind=kLoop, calls=%fused_computation.99 | loop fusion | flops 786432 | bytes 2097152 | tf_op jit(solution)/shard_map/stack | solution.py:35
  57.2 0.6 gather_fusion
  58.0 3.6 %while.13 = (s32[]{:T(128)}, f32[8,512]{1,0:T(8,128)S(1)}, f32[8,512]{1,0:T(8,128)S(1)}, f32[64,8,512]{2,1,0:T(8,128)S(1)}, f32[8,512]{1,0:T(8,128)S(1)}, /*index=5*/s32[]{:T(128)}, s32[]{:T(128)}) while((s32[]{:T(128)}, f32[8,512]{1,0:T(8,128)S(1)}, f32[8,512]{1,0:T(8,128)S(1)}, f32[64,8,512]{2,1,0:T(8,128)S(1)}, ...), condition=%wide.region_7.9_spmd.clone, body=%wide.region_5.8_spmd.clone.sunk | while | flops 1110019 | bytes 1302625 | solution.py:128
  58.2 0.1 convert_reduce_fusion.3
  58.7 0.1 convert_reduce_fusion.3
  58.9 0.1 convert_reduce_fusion.3
  59.2 0.1 convert_reduce_fusion.3
  59.4 0.1 convert_reduce_fusion.3
  59.6 0.1 convert_reduce_fusion.3
  59.8 0.1 convert_reduce_fusion.3
  60.1 0.1 convert_reduce_fusion.3
  60.3 0.1 convert_reduce_fusion.3
  61.6 0.2 fusion.22
  61.8 0.6 tile.2
  62.4 3.3 %all-to-all-start = ((f32[4,8,512]{2,1,0:T(8,128)}), f32[4,8,512]{2,1,0:T(8,128)S(1)}, u32[]{:S(2)}, u32[]{:S(2)}) async-start(f32[4,8,512]{2,1,0:T(8,128)} %tile.2), calls=%async_computation | async-start | bytes 131072 | tf_op jit(solution)/shard_map/all_to_all | solution.py:152
  65.7 5.9 %all-to-all-done = f32[4,8,512]{2,1,0:T(8,128)S(1)} async-done(((f32[4,8,512]{2,1,0:T(8,128)}), f32[4,8,512]{2,1,0:T(8,128)S(1)}, u32[]{:S(2)}, u32[]{:S(2)}) %all-to-all-start) | async-done | bytes 65568 | tf_op jit(solution)/shard_map/all_to_all | solution.py:152
  71.6 1.3 %collective-permute-start.7 = (f32[4,512]{1,0:T(4,128)S(1)}, f32[4,512]{1,0:T(4,128)S(1)}, u32[]{:S(2)}, u32[]{:S(2)}) collective-permute-start(f32[4,512]{1,0:T(4,128)S(1)} %get-tuple-element.134), channel_id=1, source_target_pairs={{2,0},{4,2},{6,4},{3,1},{5,3},{7,5},{10,8},{12,10},{14,12},{11,9},... | collective-permute-start | bytes 24584 | tf_op jit(solution)/shard_map/ppermute | solution.py:45
  72.9 3.2 %collective-permute-start.6 = (f32[4,512]{1,0:T(4,128)S(1)}, f32[4,512]{1,0:T(4,128)S(1)}, u32[]{:S(2)}, u32[]{:S(2)}) collective-permute-start(f32[4,512]{1,0:T(4,128)S(1)} %get-tuple-element.133), channel_id=1, source_target_pairs={{0,2},{2,4},{4,6},{1,3},{3,5},{5,7},{8,10},{10,12},{12,14},{9,11},... | collective-permute-start | bytes 24584 | tf_op jit(solution)/shard_map/ppermute | solution.py:44
  76.1 0.6 collective-permute-done.6
  76.8 1.3 %collective-permute-start.8 = (f32[4,40]{0,1:T(8,128)S(1)}, f32[4,40]{0,1:T(8,128)S(1)}, u32[]{:S(2)}, u32[]{:S(2)}) collective-permute-start(f32[4,40]{0,1:T(8,128)S(1)} %fusion.56), channel_id=1, source_target_pairs={{0,1},{1,0},{2,3},{3,2},{4,5},{5,4},{6,7},{7,6},{8,9},{9,8},{10,11... | collective-permute-start | bytes 1928 | tf_op jit(solution)/shard_map/ppermute | solution.py:64
  78.1 2.5 %collective-permute-done.8 = f32[4,40]{0,1:T(8,128)S(1)} collective-permute-done((f32[4,40]{0,1:T(8,128)S(1)}, f32[4,40]{0,1:T(8,128)S(1)}, u32[]{:S(2)}, u32[]{:S(2)}) %collective-permute-start.8) | collective-permute-done | bytes 672 | tf_op jit(solution)/shard_map/ppermute | solution.py:64
  80.8 0.6 multiply_add_fusion
  81.4 1.3 %fusion.45 = f32[8,32,512]{2,1,0:T(8,128)S(1)} fusion(f32[8,32,520]{2,1,0:T(8,128)S(1)} %multiply_add_fusion, f32[8]{0:T(128)S(1)} %get-tuple-element.140, f32[8]{0:T(128)S(1)} %get-tuple-element.141, f32[8]{0:T(128)S(1)} %get-tuple-element.142, f32[8]{0:T(128)S(1)} %get-tuple-element.143, f32[8]{0:T(128)S(1)} %get-tuple-element.144, ...), kind=kLoop, calls=%fused_computation.105 | loop fusion | flops 2228224 | bytes 5243168 | tf_op jit(solution)/shard_map/add | solution.py:167
  82.7 1.8 %subtract_select_fusion = f32[16,32,512]{2,1,0:T(8,128)} fusion(pred[16,32,512]{2,1,0:T(8,128)(4,1)S(1)} %get-tuple-element.109, f32[16,32,512]{2,1,0:T(8,128)S(1)} %get-tuple-element.108, f32[32,512]{1,0:T(8,128)S(1)} %get-tuple-element.117, f32[16]{0:T(128)S(1)} %get-tuple-element.149, f32[32,512]{1,0:T(8,128)S(1)} %get-tuple-element.118, ...), kind=kLoop, calls=%fused_computation.100 | loop fusion | flops 4456448 | bytes 2884096 | tf_op jit(solution)/shard_map/jit(_where)/select_n | solution.py:175
  84.5 0.6 copy.30
  (122 shorter events, 3.1 us)
Async XLA Ops:
  0.6 8.2 %copy-start = (f32[16,32,512]{2,1,0:T(8,128)S(1)}, f32[16,32,512]{2,1,0:T(8,128)}, u32[]{:S(2)}) copy-start(f32[16,32,512]{2,1,0:T(8,128)} %param.8) | copy-start | bytes 3145732
  0.6 5.8 %copy-start.5 = (s32[16,2]{0,1:T(2,128)S(1)}, s32[16,2]{0,1:T(2,128)}, u32[]{:S(2)}) copy-start(s32[16,2]{0,1:T(2,128)} %param.11) | copy-start | bytes 388
  0.7 5.9 %copy-start.6 = (s32[16,2]{0,1:T(2,128)S(1)}, s32[16,2]{0,1:T(2,128)}, u32[]{:S(2)}) copy-start(s32[16,2]{0,1:T(2,128)} %param.10) | copy-start | bytes 388
  2.1 6.8 %collective-permute-start.1 = (f32[16,11,512]{2,1,0:T(8,128)S(1)}, f32[16,11,512]{2,1,0:T(8,128)S(1)}, u32[]{:S(2)}, u32[]{:S(2)}) collective-permute-start(f32[16,11,512]{2,1,0:T(8,128)S(1)} %get-tuple-element.115), channel_id=1, source_target_pairs={{2,0},{4,2},{6,4},{3,1},{5,3},{7,5},{10,8},{12,10},{14,12},{11,9},... | collective-permute-start | bytes 1081352 | tf_op jit(solution)/shard_map/ppermute | solution.py:45
  3.4 5.5 %collective-permute-start = (f32[16,11,512]{2,1,0:T(8,128)S(1)}, f32[16,11,512]{2,1,0:T(8,128)S(1)}, u32[]{:S(2)}, u32[]{:S(2)}) collective-permute-start(f32[16,11,512]{2,1,0:T(8,128)S(1)} %get-tuple-element.114), channel_id=1, source_target_pairs={{0,2},{2,4},{4,6},{1,3},{3,5},{5,7},{8,10},{10,12},{12,14},{9,11},... | collective-permute-start | bytes 1081352 | tf_op jit(solution)/shard_map/ppermute | solution.py:44
  9.4 5.2 %collective-permute-start.2 = (f32[11,864]{1,0:T(8,128)S(1)}, f32[11,864]{1,0:T(8,128)S(1)}, u32[]{:S(2)}, u32[]{:S(2)}) collective-permute-start(f32[11,864]{1,0:T(8,128)S(1)} %reshape.216), channel_id=1, source_target_pairs={{0,1},{1,0},{2,3},{3,2},{4,5},{5,4},{6,7},{7,6},{8,9},{9,8},{10,11... | collective-permute-start | bytes 114056 | tf_op jit(solution)/shard_map/ppermute | solution.py:64
  16.4 4.2 %copy-start.1 = (s32[16,32,512]{2,1,0:T(8,128)S(1)}, s32[16,32,512]{2,1,0:T(8,128)}, u32[]{:S(2)}) copy-start(s32[16,32,512]{2,1,0:T(8,128)} %param.9) | copy-start | bytes 3145732
  28.3 8.7 %collective-permute-start.5 = (f32[16,8,512]{2,1,0:T(8,128)S(1)}, f32[16,8,512]{2,1,0:T(8,128)S(1)}, u32[]{:S(2)}, u32[]{:S(2)}) collective-permute-start(f32[16,8,512]{2,1,0:T(8,128)S(1)} %get-tuple-element.111), channel_id=1, source_target_pairs={{0,24},{8,16},{16,8},{24,0},{1,25},{9,17},{17,9},{25,1},{2,26},{10... | collective-permute-start | bytes 786440 | tf_op jit(solution)/shard_map/ppermute | solution.py:34
  32.5 22.8 %collective-permute-start.4 = (f32[16,8,512]{2,1,0:T(8,128)S(1)}, f32[16,8,512]{2,1,0:T(8,128)S(1)}, u32[]{:S(2)}, u32[]{:S(2)}) collective-permute-start(f32[16,8,512]{2,1,0:T(8,128)S(1)} %get-tuple-element.112), channel_id=1, source_target_pairs={{0,16},{8,24},{16,0},{24,8},{1,17},{9,25},{17,1},{25,9},{2,18},{10... | collective-permute-start | bytes 786440 | tf_op jit(solution)/shard_map/ppermute | solution.py:34
  32.5 22.8 %collective-permute-start.3 = (f32[16,8,512]{2,1,0:T(8,128)S(1)}, f32[16,8,512]{2,1,0:T(8,128)S(1)}, u32[]{:S(2)}, u32[]{:S(2)}) collective-permute-start(f32[16,8,512]{2,1,0:T(8,128)S(1)} %get-tuple-element.113), channel_id=1, source_target_pairs={{0,8},{8,0},{16,24},{24,16},{1,9},{9,1},{17,25},{25,17},{2,10},{10... | collective-permute-start | bytes 786440 | tf_op jit(solution)/shard_map/ppermute | solution.py:34
  37.0 18.2 %copy-start.2 = (f32[16,8,512]{2,1,0:T(8,128)}, f32[16,8,512]{2,1,0:T(8,128)S(1)}, u32[]{:S(2)}) copy-start(f32[16,8,512]{2,1,0:T(8,128)S(1)} %collective-permute-done.5) | copy-start | bytes 786436
  55.3 0.7 copy-start.3
  55.3 0.8 copy-start.4
  61.6 14.5 %copy-start.7 = (s32[16]{0:T(128)S(1)}, s32[16]{0:T(128)}, u32[]{:S(2)}) copy-start(s32[16]{0:T(128)} %param.12) | copy-start | bytes 196
  62.4 9.2 %all-to-all-start = ((f32[4,8,512]{2,1,0:T(8,128)}), f32[4,8,512]{2,1,0:T(8,128)S(1)}, u32[]{:S(2)}, u32[]{:S(2)}) async-start(f32[4,8,512]{2,1,0:T(8,128)} %tile.2), calls=%async_computation | async-start | bytes 131072 | tf_op jit(solution)/shard_map/all_to_all | solution.py:152
  71.6 4.5 %collective-permute-start.7 = (f32[4,512]{1,0:T(4,128)S(1)}, f32[4,512]{1,0:T(4,128)S(1)}, u32[]{:S(2)}, u32[]{:S(2)}) collective-permute-start(f32[4,512]{1,0:T(4,128)S(1)} %get-tuple-element.134), channel_id=1, source_target_pairs={{2,0},{4,2},{6,4},{3,1},{5,3},{7,5},{10,8},{12,10},{14,12},{11,9},... | collective-permute-start | bytes 24584 | tf_op jit(solution)/shard_map/ppermute | solution.py:45
  72.9 3.8 %collective-permute-start.6 = (f32[4,512]{1,0:T(4,128)S(1)}, f32[4,512]{1,0:T(4,128)S(1)}, u32[]{:S(2)}, u32[]{:S(2)}) collective-permute-start(f32[4,512]{1,0:T(4,128)S(1)} %get-tuple-element.133), channel_id=1, source_target_pairs={{0,2},{2,4},{4,6},{1,3},{3,5},{5,7},{8,10},{10,12},{12,14},{9,11},... | collective-permute-start | bytes 24584 | tf_op jit(solution)/shard_map/ppermute | solution.py:44
  76.8 3.8 %collective-permute-start.8 = (f32[4,40]{0,1:T(8,128)S(1)}, f32[4,40]{0,1:T(8,128)S(1)}, u32[]{:S(2)}, u32[]{:S(2)}) collective-permute-start(f32[4,40]{0,1:T(8,128)S(1)} %fusion.56), channel_id=1, source_target_pairs={{0,1},{1,0},{2,3},{3,2},{4,5},{5,4},{6,7},{7,6},{8,9},{9,8},{10,11... | collective-permute-start | bytes 1928 | tf_op jit(solution)/shard_map/ppermute | solution.py:64
